TPU v7x, 256 devices: a whole 4x4x8 slice. The times are simulated.
256 devices in a mesh: dp: 4 (over x), seq: 4 (over y_hi, core), tensor: 16 (over y_lo, z).
Axes of the slice: x: 4, y: 4 (y_hi: 2, y_lo: 2; y = y_hi * 2 + y_lo), z: 8, core: 2. Of those that a mesh axis runs over, the one named last changes fastest.
Arguments:
- byte_acts: bfloat16 [4, 16384, 2048], P('dp', 'seq', 'tensor'), may hold values from -18 to 18
- conv_weight: bfloat16 [16, 1024, 128], P('tensor'), may hold values from -0.1875 to 0.1875
- conv_bias: float32 [2048], P('tensor'), may hold values from -3 to 3
- proj_weight: bfloat16 [2048, 8192], P(None, 'tensor'), may hold values from -0.125 to 0.125
- teacher: bfloat16 [4, 4096, 8192], P('dp', 'seq', 'tensor'), may hold values from -6 to 6
- span_lengths: int32 [4, 4096], P('dp'), may hold values from 1 to 16, as said below
Outputs:
- downsampled: bfloat16 [4, 4096, 2048], P('dp', 'seq', 'tensor')
- byte_grad: bfloat16 [4, 16384, 2048], P('dp', 'seq', 'tensor')
- conv_grad: float32 [16, 1024, 128], P('tensor')
- proj_grad: float32 [2048, 8192], P(None, 'tensor')
Inputs may be any that keep to these rules, and one draw needn't show every extreme that they name: `span_lengths`: each document's 4096 span lengths cover its 16384 bytes in order; the longest is exactly 16.
All inputs are finite; a program needn't handle non-finite values.
Results may differ from a plain program's by a relative error of at most 0.019.
Values may be sent and summed in bfloat16 or wider, within the bound.
No kernel may reach another device: no remote copies, remote signals or barrier semaphores. Data moves between devices by JAX's collectives and lax.ppermute only.
A program may use at most 64 MiB of HBM per device.

v0:
```python
import jax
import jax.numpy as jnp
from jax import lax
from jax.sharding import PartitionSpec as P

STRIDE = 4
KERNEL = 8


def shifted(block, axis, distance):
    devices = range(lax.axis_size(axis))
    route = [(i - distance, i) for i in devices if i - distance in devices]
    return lax.ppermute(block, axis, route)


def intersection_weights(span_start, span_end, span_lengths, first_position, position_count):
    byte_first = (first_position + jnp.arange(position_count, dtype=jnp.int32)) * STRIDE
    lower_edge = jnp.maximum(span_start[:, None], byte_first[None, :])
    upper_edge = jnp.minimum(span_end[:, None], byte_first[None, :] + STRIDE)
    covered = jnp.maximum(upper_edge - lower_edge, 0).astype(jnp.float32)
    return (covered / span_lengths[:, None].astype(jnp.float32)).astype(jnp.bfloat16)


def local(byte_acts, conv_weight, conv_bias, proj_weight, teacher, span_lengths):
    byte_rows = byte_acts[0]
    row_total, width = byte_rows.shape
    groups_here = conv_weight.shape[0]
    group_width = width // groups_here
    positions = row_total // STRIDE
    seq_count = lax.axis_size("seq")
    seq_rank = lax.axis_index("seq")
    lengths_doc = span_lengths[0]
    tokens_all = lengths_doc.shape[0]
    span_end = jnp.cumsum(lengths_doc)
    span_start = span_end - lengths_doc
    next_rows = shifted(byte_rows[:STRIDE], "seq", -1)
    extended = jnp.concatenate([byte_rows, next_rows], axis=0)
    blocks = extended.reshape(positions + 1, STRIDE, groups_here, group_width)
    windows = jnp.concatenate([blocks[:-1], blocks[1:]], axis=1)
    taps_weight = conv_weight.reshape(groups_here, KERNEL, group_width, group_width)
    conv_out = jnp.einsum(
        "pkgc,gkco->pgo", windows, taps_weight, preferred_element_type=jnp.float32
    )
    conv_out = conv_out + conv_bias.reshape(groups_here, group_width)[None]
    downsampled = conv_out.reshape(positions, width).astype(jnp.bfloat16)
    local_weight = intersection_weights(
        span_start, span_end, lengths_doc, seq_rank * positions, positions
    )
    weight_part = local_weight
    pooled_sum = lax.psum_scatter(
        jnp.dot(weight_part, downsampled, preferred_element_type=jnp.float32).astype(jnp.bfloat16),
        "seq",
        scatter_dimension=0,
        tiled=True,
    )
    gathered = lax.all_gather(pooled_sum, "tensor", axis=1, tiled=True)
    predicted = jnp.dot(gathered, proj_weight, preferred_element_type=jnp.float32)
    err_grad = (predicted - teacher[0].astype(jnp.float32)).astype(jnp.bfloat16)
    proj_local = lax.dot_general(
        gathered, err_grad, (((0,), (0,)), ((), ())), preferred_element_type=jnp.float32
    )
    token_scale = 1.0 / jnp.sqrt(jnp.float32(lax.axis_size("dp") * tokens_all))
    proj_summed = lax.psum(proj_local.astype(jnp.bfloat16), ("dp", "seq")).astype(jnp.float32)
    proj_grad = proj_summed * token_scale
    weight_part = proj_weight
    pooled_grad_t = lax.psum_scatter(
        lax.dot_general(
            weight_part, err_grad, (((1,), (1,)), ((), ())), preferred_element_type=jnp.float32
        ).astype(jnp.bfloat16),
        "tensor",
        scatter_dimension=0,
        tiled=True,
    )
    weight_part = local_weight
    down_sum = lax.dot_general(
        weight_part,
        lax.all_gather(pooled_grad_t, "seq", axis=1, tiled=True),
        (((0,), (1,)), ((), ())),
        preferred_element_type=jnp.float32,
    )
    down_grad = down_sum.astype(jnp.bfloat16).reshape(positions, groups_here, group_width)
    conv_local = jnp.einsum(
        "pkgc,pgo->gkco", windows, down_grad, preferred_element_type=jnp.float32
    )
    conv_summed = lax.psum(conv_local.astype(jnp.bfloat16), ("dp", "seq")).astype(jnp.float32)
    position_scale = 1.0 / jnp.sqrt(jnp.float32(lax.axis_size("dp") * positions * seq_count))
    conv_grad = (conv_summed * position_scale).reshape(
        groups_here, KERNEL * group_width, group_width
    )
    window_grad = jnp.einsum(
        "pgo,gkco->pkgc", down_grad, taps_weight, preferred_element_type=jnp.float32
    )
    incoming = shifted(window_grad[-1, STRIDE:], "seq", 1)
    carried_grad = jnp.concatenate([incoming[None], window_grad[:-1, STRIDE:]], axis=0)
    byte_grad = (
        (window_grad[:, :STRIDE] + carried_grad).reshape(row_total, width).astype(jnp.bfloat16)
    )
    return (downsampled[None], byte_grad[None], conv_grad, proj_grad)


def solution(mesh):
    return jax.shard_map(
        local,
        mesh=mesh,
        in_specs=(
            P("dp", "seq", "tensor"),
            P("tensor", None, None),
            P("tensor"),
            P(None, "tensor"),
            P("dp", "seq", "tensor"),
            P("dp", None),
        ),
        out_specs=(
            P("dp", "seq", "tensor"),
            P("dp", "seq", "tensor"),
            P("tensor", None, None),
            P(None, "tensor"),
        ),
        check_vma=False,
    )
```

profile of v0, /device:TPU:1, one launch (start us, length us, event | category | flops | bytes accessed | tf_op | source)
XLA Modules:
  0.0 448.6 jit_solution(9548664783384587583)
XLA Ops:
  7.2 0.0 copy-start
  7.2 0.0 copy-start.6
  7.2 0.0 copy-start.3
  7.2 0.0 reduce-scatter.5.cloned.1.call-start
  7.2 0.8 slice_bitcast_fusion
  8.1 5.1 %collective-permute-start = (bf16[4,128]{1,0:T(4,128)(2,1)S(1)}, bf16[4,128]{1,0:T(4,128)(2,1)S(1)}, u32[]{:S(2)}, u32[]{:S(2)}) collective-permute-start(bf16[4,128]{1,0:T(4,128)(2,1)S(1)} %slice_bitcast_fusion), channel_id=1, source_target_pairs={{16,0},{32,16},{48,32},{17,1},{33,17},{49,33},{18,2},{34,18},{50,3... | collective-permute-start | bytes 3080 | tf_op jit(solution)/shard_map/ppermute | solution.py:13
  13.2 1.0 reduce-window.9
  14.2 0.1 slice.42
  14.3 0.1 reduce-window.12
  14.4 0.1 slice_reduce_fusion
  14.5 0.8 fusion.23
  15.3 0.7 convert_element_type.87
  16.0 1.4 copy.17
  17.4 0.0 collective-permute-done
  17.4 1.5 pad_maximum_fusion
  18.9 0.1 copy.18
  19.0 0.0 copy-start.1
  19.1 1.0 copy-done.1
  20.0 0.0 copy-done.6
  20.0 0.0 copy-done.3
  20.0 0.7 fusion.11
  20.7 0.0 copy-start.7
  20.8 0.7 copy-done.7
  21.5 7.5 %fusion.2 = bf16[4096,128]{1,0:T(8,128)(2,1)} fusion(f32[4096]{0:T(1024)S(1)} %convert_element_type.87, s32[1024]{0:T(1024)S(1)} %add_multiply_fusion, s32[4096]{0:T(1024)S(1)} %get-tuple-element.6, s32[1024]{0:T(1024)S(1)} %broadcast_add_fusion, s32[4096]{0:T(1024)S(1)} %get-tuple-element.7, bf16[1,128,1024]{1,2,0:T(8,128)(2,1)S(1)} %fusion.11), kind=kOutput, calls=%fused_computation.3 | convolution fusion | flops 1103626240 | bytes 1368064 | tf_op jit(solution)/shard_map/dot_general | solution.py:51
  29.0 0.0 reduce-scatter.5.cloned.1.call-update
  29.0 0.0 all-gather.3.cloned.1.call-start
  29.0 38.1 %reduce-scatter.5.cloned.1.call-done = bf16[1024,128]{1,0:T(8,128)(2,1)} async-done(((bf16[4096,128]{1,0:T(8,128)(2,1)}), bf16[1024,128]{1,0:T(8,128)(2,1)}) %reduce-scatter.5.cloned.1.call-update) | async-done | bytes 262160 | tf_op jit(solution)/shard_map/reduce_scatter | solution.py:50
  67.2 0.0 all-gather.3.cloned.1.call-update
  67.2 0.0 reduce-scatter.7.cloned.1.call-start
  67.2 80.8 %all-gather.3.cloned.1.call-done = bf16[1024,2048]{1,0:T(8,128)(2,1)} async-done(((bf16[1024,128]{1,0:T(8,128)(2,1)}), bf16[1024,2048]{1,0:T(8,128)(2,1)}) %all-gather.3.cloned.1.call-update) | async-done | bytes 4194320 | tf_op jit(solution)/shard_map/all_gather | solution.py:56
  148.1 0.0 copy-done
  148.1 0.0 copy-start.5
  148.1 4.6 %fusion.24 = f32[1024,512]{1,0:T(8,128)S(1)} fusion(bf16[1024,2048]{1,0:T(8,128)(2,1)} %all-gather.3.cloned.1.call-done, bf16[2048,512]{1,0:T(8,128)(2,1)S(1)} %copy-done), kind=kOutput, calls=%fused_computation.37 | convolution fusion | flops 2147483648 | bytes 8388608 | tf_op jit(solution)/shard_map/dot_general | solution.py:57
  152.7 0.0 copy-start.8
  152.7 1.4 copy-done.8
  154.0 0.0 copy-done.5
  154.0 4.4 convert_bitcast_fusion
  158.4 6.4 %copy.23 = bf16[2048,1024]{1,0:T(8,128)(2,1)} copy(bf16[2048,1024]{0,1:T(8,128)(2,1)} %convert_bitcast_fusion) | data formatting | bytes 8388608
  164.9 0.0 reduce-scatter.7.cloned.1.call-update
  164.9 0.0 all-gather.5.cloned.1.call-start
  164.9 78.6 %reduce-scatter.7.cloned.1.call-done = bf16[128,1024]{1,0:T(8,128)(2,1)} async-done(((bf16[2048,1024]{1,0:T(8,128)(2,1)}), bf16[128,1024]{1,0:T(8,128)(2,1)}) %reduce-scatter.7.cloned.1.call-update) | async-done | bytes 262160
  243.5 1.8 copy.24
  245.3 0.0 all-gather.5.cloned.1.call-update
  245.3 0.2 all-reduce.3.cloned.1.call-start
  245.6 6.8 %convolution_convert_fusion = bf16[2048,512]{1,0:T(8,128)(2,1)} fusion(bf16[1024,2048]{1,0:T(8,128)(2,1)} %all-gather.3.cloned.1.call-done, f32[1024,512]{1,0:T(8,128)} %copy-done.8, bf16[1,1024,512]{2,1,0:T(8,128)(2,1)} %param.10), kind=kOutput, calls=%fused_computation.6 | convolution fusion | flops 2150105088 | bytes 9437184 | tf_op jit(solution)/shard_map/dot_general | solution.py:59
  252.3 24.2 %all-gather.5.cloned.1.call-done = bf16[128,4096]{0,1:T(8,128)(2,1)} async-done(((bf16[128,1024]{0,1:T(8,128)(2,1)}), bf16[128,4096]{0,1:T(8,128)(2,1)}) %all-gather.5.cloned.1.call-update) | async-done | bytes 1048592 | tf_op jit(solution)/shard_map/all_gather | solution.py:77
  276.5 0.0 copy-start.2
  276.5 7.7 %fusion.15 = bf16[1024,128,1]{1,0,2:T(8,128)(2,1)S(1)} fusion(bf16[128,4096]{0,1:T(8,128)(2,1)} %all-gather.5.cloned.1.call-done, f32[4096]{0:T(1024)S(1)} %convert_element_type.87, s32[1024]{0:T(1024)S(1)} %add_multiply_fusion, s32[4096]{0:T(1024)S(1)} %get-tuple-element.6, s32[1024]{0:T(1024)S(1)} %broadcast_add_fusion, s32[4096]{0:T(1024)S(1)} %get-tuple-element.7), kind=kOutput, calls=%fused_computation.21 | convolution fusion | flops 1103233024 | bytes 1368064 | tf_op jit(solution)/shard_map/dot_general | solution.py:75
  284.2 0.0 copy-start.4
  284.2 0.7 copy-done.4
  284.9 0.0 copy-done.2
  284.9 1.4 fusion.14
  286.3 0.0 all-reduce.3.cloned.1.call-update
  286.4 1.7 convolution_bitcast_fusion
  288.1 2.1 collective-permute-start.1
  290.1 0.1 slice.46
  290.3 0.8 collective-permute-done.1
  291.1 0.3 fusion.3
  291.4 1.8 copy.20
  293.2 142.9 %all-reduce.3.cloned.1.call-done = (bf16[1,8,128,128]{3,2,1,0:T(8,128)(2,1)}, bf16[2048,512]{1,0:T(8,128)(2,1)}) async-done(((bf16[1,8,128,128]{3,2,1,0:T(8,128)(2,1)}, bf16[2048,512]{1,0:T(8,128)(2,1)}), (bf16[1,8,128,128]{3,2,1,0:T(8,128)(2,1)}, bf16[2048,512]{1,0:T(8,128)(2,1)})) %all-reduce.3.cloned.1.call-update) | async-done | bytes 2359312 | tf_op jit(solution)/shard_map/psum | solution.py:85
  436.1 1.8 convert_multiply_fusion.1
  437.9 4.2 convert_multiply_fusion
  (3 shorter events, 0.0 us)
Async XLA Ops:
  7.2 140.9 %copy-start = (bf16[2048,512]{1,0:T(8,128)(2,1)S(1)}, bf16[2048,512]{1,0:T(8,128)(2,1)}, u32[]{:S(2)}) copy-start(bf16[2048,512]{1,0:T(8,128)(2,1)} %param.9) | copy-start | bytes 6291460
  7.2 12.8 %copy-start.6 = (f32[128]{0:T(128)S(1)}, f32[128]{0:T(128)}, u32[]{:S(2)}) copy-start(f32[128]{0:T(128)} %param.8) | copy-start | bytes 1540
  7.2 12.8 %copy-start.3 = (bf16[1,1024,128]{2,1,0:T(8,128)(2,1)S(1)}, bf16[1,1024,128]{2,1,0:T(8,128)(2,1)}, u32[]{:S(2)}) copy-start(bf16[1,1024,128]{2,1,0:T(8,128)(2,1)} %param.7) | copy-start | bytes 786436
  7.2 60.0 %reduce-scatter.5.cloned.1.call-start = ((), (), s32[]{:S(2)}) async-start(), calls=%async_computation.2 | async-start | bytes 1310720 | tf_op jit(solution)/shard_map/reduce_scatter | solution.py:50
  8.1 9.3 %collective-permute-start = (bf16[4,128]{1,0:T(4,128)(2,1)S(1)}, bf16[4,128]{1,0:T(4,128)(2,1)S(1)}, u32[]{:S(2)}, u32[]{:S(2)}) collective-permute-start(bf16[4,128]{1,0:T(4,128)(2,1)S(1)} %slice_bitcast_fusion), channel_id=1, source_target_pairs={{16,0},{32,16},{48,32},{17,1},{33,17},{49,33},{18,2},{34,18},{50,3... | collective-permute-start | bytes 3080 | tf_op jit(solution)/shard_map/ppermute | solution.py:13
  19.0 1.0 copy-start.1
  20.7 0.7 copy-start.7
  29.0 119.1 %all-gather.3.cloned.1.call-start = ((), (), s32[]{:S(2)}) async-start(), calls=%async_computation.3 | async-start | bytes 4456448 | tf_op jit(solution)/shard_map/all_gather | solution.py:56
  67.2 176.3 %reduce-scatter.7.cloned.1.call-start = ((), (), s32[]{:S(2)}) async-start(), calls=%async_computation.5 | async-start | bytes 4456448
  148.1 6.0 %copy-start.5 = (bf16[1,1024,512]{2,1,0:T(8,128)(2,1)S(1)}, bf16[1,1024,512]{2,1,0:T(8,128)(2,1)}, u32[]{:S(2)}) copy-start(bf16[1,1024,512]{2,1,0:T(8,128)(2,1)} %param.10) | copy-start | bytes 3145732
  152.7 1.4 copy-start.8
  164.9 111.6 %all-gather.5.cloned.1.call-start = ((), (), s32[]{:S(2)}) async-start(), calls=%async_computation.4 | async-start | bytes 1310720 | tf_op jit(solution)/shard_map/all_gather | solution.py:77
  245.3 190.8 %all-reduce.3.cloned.1.call-start = ((), (), s32[]{:S(2)}) async-start(), calls=%async_computation.6 | async-start | bytes 4718592 | tf_op jit(solution)/shard_map/psum | solution.py:85
  276.5 8.4 %copy-start.2 = (bf16[1024,4,1,128]{3,0,1,2:T(8,128)(2,1)S(1)}, bf16[1024,4,1,128]{3,0,1,2:T(8,128)(2,1)}, u32[]{:S(2)}) copy-start(bf16[1024,4,1,128]{3,0,1,2:T(8,128)(2,1)} %copy-done.1) | copy-start | bytes 3145732
  284.2 0.7 copy-start.4
  288.1 3.1 collective-permute-start.1
Sparse Core Ops, SparseCore 0:
  29.1 38.0 reduce-scatter.4
  69.0 79.0 all-gather.2
  165.0 78.4 reduce-scatter.6
  245.9 30.5 all-gather.4
  286.5 149.5 all-reduce.2
where the time goes:
time: 449 us
  waiting for transfers between devices  366 us (82%)
  matrix products  34.8 us (8%)
  local copies, waits for them, and re-layouts  16.4 us (4%)
  between operations  13.9 us (3%)
  other arithmetic  10.3 us (2%)
  starting transfers between devices  7.58 us (2%)
    psum x1, waiting for transfers between devices, local(): lax.psum(conv_local.astype(jnp.bfloat16), ('dp', 'seq')).astype(jnp.float32)  143 us
    all_gather x1, waiting for transfers between devices, local(): gathered = lax.all_gather(pooled_sum, 'tensor', axis=1, tiled=True)  80.8 us
    unnamed x6, waiting for transfers between devices  78.7 us
    reduce_scatter x1, waiting for transfers between devices, local(): lax.psum_scatter(jnp.dot(weight_part, downsampled, preferred_element_type...  38.1 us
    all_gather x1, waiting for transfers between devices, local(): lax.all_gather(pooled_grad_t, 'seq', axis=1, tiled=True)  24.2 us
    unnamed x20, local copies, waits for them, and re-layouts  12 us
  transfers between devices with their start and end apart: 7, of which 6 were waited for; matrix products, arithmetic and copies ran while one was open for 3% of the time, Pallas kernels for 0%

commit v1 on v0

--- a/solution.py
+++ b/solution.py
@@ -82,7 +82,9 @@
     conv_local = jnp.einsum(
         "pkgc,pgo->gkco", windows, down_grad, preferred_element_type=jnp.float32
     )
-    conv_summed = lax.psum(conv_local.astype(jnp.bfloat16), ("dp", "seq")).astype(jnp.float32)
+    conv_summed = lax.psum(lax.psum(conv_local.astype(jnp.bfloat16), "dp"), "seq").astype(
+        jnp.float32
+    )
     position_scale = 1.0 / jnp.sqrt(jnp.float32(lax.axis_size("dp") * positions * seq_count))
     conv_grad = (conv_summed * position_scale).reshape(
         groups_here, KERNEL * group_width, group_width

time: 449 us -> 538 us (1.20)
  waiting for transfers between devices: 366 us -> 450 us
    psum x1 -> x3, waiting for transfers between devices: 143 us -> 228 us  [the longest x1 138 us: local(): lax.psum(proj_local.astype(jnp.bfloat16), ('dp', 'seq')).astype(jnp.float32)]
    unnamed x20 -> x22, local copies, waits for them, and re-layouts: 12 us -> 13.2 us
    unnamed x6 -> x8, waiting for transfers between devices: 78.7 us -> 78.6 us
  transfers between devices with their start and end apart: 7 -> 9, of which waited for: 6 -> 7; matrix products, arithmetic and copies ran while one was open for 3% -> 6% of each run, Pallas kernels for 0% -> 0%
where the time goes in v1:
time: 538 us; the launch traced here: 537 us
  waiting for transfers between devices  450 us (84%)
  matrix products  33.7 us (6%)
  local copies, waits for them, and re-layouts  19 us (4%)
  between operations  14.3 us (3%)
  other arithmetic  12.7 us (2%)
  starting transfers between devices  7.65 us (1%)
    psum x1, waiting for transfers between devices, local(): lax.psum(proj_local.astype(jnp.bfloat16), ('dp', 'seq')).astype(jnp.float32)  138 us
    all_gather x1, waiting for transfers between devices, local(): gathered = lax.all_gather(pooled_sum, 'tensor', axis=1, tiled=True)  80.8 us
    unnamed x8, waiting for transfers between devices  78.6 us
    psum x1, waiting for transfers between devices, local(): lax.psum(lax.psum(conv_local.astype(jnp.bfloat16), 'dp'), 'seq')  47.1 us
    psum x1, waiting for transfers between devices, local(): lax.psum(conv_local.astype(jnp.bfloat16), 'dp')  43 us
    reduce_scatter x1, waiting for transfers between devices, local(): lax.psum_scatter(jnp.dot(weight_part, downsampled, preferred_element_type...  38.1 us
    all_gather x1, waiting for transfers between devices, local(): lax.all_gather(pooled_grad_t, 'seq', axis=1, tiled=True)  24.6 us
    unnamed x22, local copies, waits for them, and re-layouts  13.2 us
  transfers between devices with their start and end apart: 9, of which 7 were waited for; matrix products, arithmetic and copies ran while one was open for 6% of the time, Pallas kernels for 0%

profile of v1, /device:TPU:1, one launch (start us, length us, event | category | flops | bytes accessed | tf_op | source)
XLA Modules:
  0.0 537.3 jit_solution(16697866251638116711)
XLA Ops:
  7.2 0.0 copy-start
  7.2 0.0 copy-start.7
  7.2 0.0 copy-start.5
  7.2 0.0 reduce-scatter.5.cloned.1.call-start
  7.2 0.8 slice_bitcast_fusion
  8.1 5.1 collective-permute-start
  13.2 1.0 reduce-window.9
  14.2 0.1 slice.42
  14.3 0.1 reduce-window.12
  14.4 0.1 slice_reduce_fusion
  14.5 0.8 fusion.23
  15.3 0.7 convert_element_type.87
  16.0 1.4 copy.17
  17.4 0.0 collective-permute-done
  17.4 1.5 pad_maximum_fusion
  18.9 0.1 copy.18
  19.0 0.0 copy-start.3
  19.1 1.0 copy-done.3
  20.0 0.0 copy-done.7
  20.0 0.0 copy-done.5
  20.0 0.7 fusion.11
  20.8 0.0 copy-start.8
  20.8 0.7 copy-done.8
  21.5 7.5 %fusion.2 = bf16[4096,128]{1,0:T(8,128)(2,1)} fusion(f32[4096]{0:T(1024)S(1)} %convert_element_type.87, s32[1024]{0:T(1024)S(1)} %add_multiply_fusion, s32[4096]{0:T(1024)S(1)} %get-tuple-element.4, s32[1024]{0:T(1024)S(1)} %broadcast_add_fusion, s32[4096]{0:T(1024)S(1)} %get-tuple-element.5, bf16[1,128,1024]{1,2,0:T(8,128)(2,1)S(1)} %fusion.11), kind=kOutput, calls=%fused_computation.3 | convolution fusion | flops 1103626240 | bytes 1368064 | tf_op jit(solution)/shard_map/dot_general | solution.py:51
  29.0 0.0 reduce-scatter.5.cloned.1.call-update
  29.0 0.0 all-gather.3.cloned.1.call-start
  29.1 38.1 %reduce-scatter.5.cloned.1.call-done = bf16[1024,128]{1,0:T(8,128)(2,1)} async-done(((bf16[4096,128]{1,0:T(8,128)(2,1)}), bf16[1024,128]{1,0:T(8,128)(2,1)}) %reduce-scatter.5.cloned.1.call-update) | async-done | bytes 262160 | tf_op jit(solution)/shard_map/reduce_scatter | solution.py:50
  67.2 0.0 all-gather.3.cloned.1.call-update
  67.2 0.0 reduce-scatter.7.cloned.1.call-start
  67.3 80.8 %all-gather.3.cloned.1.call-done = bf16[1024,2048]{1,0:T(8,128)(2,1)} async-done(((bf16[1024,128]{1,0:T(8,128)(2,1)}), bf16[1024,2048]{1,0:T(8,128)(2,1)}) %all-gather.3.cloned.1.call-update) | async-done | bytes 4194320 | tf_op jit(solution)/shard_map/all_gather | solution.py:56
  148.1 0.0 copy-done
  148.1 4.6 fusion.24
  152.7 0.0 copy-start.9
  152.7 1.4 copy-done.9
  154.0 0.0 copy-done.6
  154.0 4.4 convert_bitcast_fusion
  158.4 6.4 %copy.23 = bf16[2048,1024]{1,0:T(8,128)(2,1)} copy(bf16[2048,1024]{0,1:T(8,128)(2,1)} %convert_bitcast_fusion) | data formatting | bytes 8388608
  164.9 0.0 reduce-scatter.7.cloned.1.call-update
  164.9 0.0 all-gather.5.cloned.1.call-start
  164.9 78.5 %reduce-scatter.7.cloned.1.call-done = bf16[128,1024]{1,0:T(8,128)(2,1)} async-done(((bf16[2048,1024]{1,0:T(8,128)(2,1)}), bf16[128,1024]{1,0:T(8,128)(2,1)}) %reduce-scatter.7.cloned.1.call-update) | async-done | bytes 262160
  243.4 1.8 copy.24
  245.2 0.0 all-gather.5.cloned.1.call-update
  245.2 0.0 all-reduce.8.cloned.1.call-start
  245.3 6.8 %convolution_convert_fusion = bf16[2048,512]{1,0:T(8,128)(2,1)} fusion(bf16[1024,2048]{1,0:T(8,128)(2,1)} %all-gather.3.cloned.1.call-done, f32[1024,512]{1,0:T(8,128)} %copy-done.9, bf16[1,1024,512]{2,1,0:T(8,128)(2,1)} %param.10), kind=kOutput, calls=%fused_computation.6 | convolution fusion | flops 2150105088 | bytes 9437184 | tf_op jit(solution)/shard_map/dot_general | solution.py:59
  252.0 0.0 all-reduce.8.cloned.1.call-update
  252.1 0.2 all-reduce.4.cloned.1.call-start
  252.3 24.6 %all-gather.5.cloned.1.call-done = bf16[128,4096]{0,1:T(8,128)(2,1)} async-done(((bf16[128,1024]{0,1:T(8,128)(2,1)}), bf16[128,4096]{0,1:T(8,128)(2,1)}) %all-gather.5.cloned.1.call-update) | async-done | bytes 1048592 | tf_op jit(solution)/shard_map/all_gather | solution.py:77
  276.9 7.6 %fusion.15 = bf16[1024,128,1]{1,0,2:T(8,128)(2,1)S(1)} fusion(bf16[128,4096]{0,1:T(8,128)(2,1)} %all-gather.5.cloned.1.call-done, f32[4096]{0:T(1024)S(1)} %convert_element_type.87, s32[1024]{0:T(1024)S(1)} %add_multiply_fusion, s32[4096]{0:T(1024)S(1)} %get-tuple-element.4, s32[1024]{0:T(1024)S(1)} %broadcast_add_fusion, s32[4096]{0:T(1024)S(1)} %get-tuple-element.5), kind=kOutput, calls=%fused_computation.21 | convolution fusion | flops 1103233024 | bytes 1368064 | tf_op jit(solution)/shard_map/dot_general | solution.py:75
  284.5 0.7 convolution_bitcast_fusion
  285.2 1.9 copy-done.1
  287.2 2.1 collective-permute-start.1
  289.2 1.5 fusion.14
  290.7 0.0 all-reduce.4.cloned.1.call-update
  290.7 0.0 all-reduce.6.cloned.1.call-start
  290.8 137.6 %all-reduce.8.cloned.1.call-done = bf16[2048,512]{1,0:T(8,128)(2,1)} async-done(((bf16[2048,512]{1,0:T(8,128)(2,1)}), bf16[2048,512]{1,0:T(8,128)(2,1)}) %all-reduce.8.cloned.1.call-update) | async-done | bytes 2097168 | tf_op jit(solution)/shard_map/psum | solution.py:63
  428.4 4.3 convert_multiply_fusion
  432.8 1.5 slice.46
  434.2 43.0 %all-reduce.4.cloned.1.call-done = bf16[1,8,128,128]{3,2,1,0:T(8,128)(2,1)} async-done(((bf16[1,8,128,128]{3,2,1,0:T(8,128)(2,1)}), bf16[1,8,128,128]{3,2,1,0:T(8,128)(2,1)}) %all-reduce.4.cloned.1.call-update) | async-done | bytes 262160 | tf_op jit(solution)/shard_map/psum | solution.py:85
  477.3 0.0 all-reduce.6.cloned.1.call-update
  477.3 0.0 collective-permute-done.1
  477.3 2.5 fusion.3
  479.8 1.8 copy.20
  481.6 47.1 %all-reduce.6.cloned.1.call-done = bf16[1,8,128,128]{3,2,1,0:T(8,128)(2,1)} async-done(((bf16[1,8,128,128]{3,2,1,0:T(8,128)(2,1)}), bf16[1,8,128,128]{3,2,1,0:T(8,128)(2,1)}) %all-reduce.6.cloned.1.call-update) | async-done | bytes 262160 | tf_op jit(solution)/shard_map/psum | solution.py:85
  528.7 1.8 convert_multiply_fusion.1
  (9 shorter events, 0.0 us)
Async XLA Ops:
  7.2 140.9 %copy-start = (bf16[2048,512]{1,0:T(8,128)(2,1)S(1)}, bf16[2048,512]{1,0:T(8,128)(2,1)}, u32[]{:S(2)}) copy-start(bf16[2048,512]{1,0:T(8,128)(2,1)} %param.9) | copy-start | bytes 6291460
  7.2 12.9 %copy-start.7 = (f32[128]{0:T(128)S(1)}, f32[128]{0:T(128)}, u32[]{:S(2)}) copy-start(f32[128]{0:T(128)} %param.8) | copy-start | bytes 1540
  7.2 12.8 %copy-start.5 = (bf16[1,1024,128]{2,1,0:T(8,128)(2,1)S(1)}, bf16[1,1024,128]{2,1,0:T(8,128)(2,1)}, u32[]{:S(2)}) copy-start(bf16[1,1024,128]{2,1,0:T(8,128)(2,1)} %param.7) | copy-start | bytes 786436
  7.2 60.0 %reduce-scatter.5.cloned.1.call-start = ((), (), s32[]{:S(2)}) async-start(), calls=%async_computation.2 | async-start | bytes 1310720 | tf_op jit(solution)/shard_map/reduce_scatter | solution.py:50
  8.1 9.3 %collective-permute-start = (bf16[4,128]{1,0:T(4,128)(2,1)S(1)}, bf16[4,128]{1,0:T(4,128)(2,1)S(1)}, u32[]{:S(2)}, u32[]{:S(2)}) collective-permute-start(bf16[4,128]{1,0:T(4,128)(2,1)S(1)} %slice_bitcast_fusion), channel_id=1, source_target_pairs={{16,0},{32,16},{48,32},{17,1},{33,17},{49,33},{18,2},{34,18},{50,3... | collective-permute-start | bytes 3080 | tf_op jit(solution)/shard_map/ppermute | solution.py:13
  19.0 1.0 copy-start.3
  20.8 0.7 copy-start.8
  29.0 119.1 %all-gather.3.cloned.1.call-start = ((), (), s32[]{:S(2)}) async-start(), calls=%async_computation.3 | async-start | bytes 4456448 | tf_op jit(solution)/shard_map/all_gather | solution.py:56
  67.2 176.2 %reduce-scatter.7.cloned.1.call-start = ((), (), s32[]{:S(2)}) async-start(), calls=%async_computation.8 | async-start | bytes 4456448
  148.1 6.0 %copy-start.6 = (bf16[1,1024,512]{2,1,0:T(8,128)(2,1)S(1)}, bf16[1,1024,512]{2,1,0:T(8,128)(2,1)}, u32[]{:S(2)}) copy-start(bf16[1,1024,512]{2,1,0:T(8,128)(2,1)} %param.10) | copy-start | bytes 3145732
  152.7 1.4 copy-start.9
  164.9 112.0 %all-gather.5.cloned.1.call-start = ((), (), s32[]{:S(2)}) async-start(), calls=%async_computation.4 | async-start | bytes 1310720 | tf_op jit(solution)/shard_map/all_gather | solution.py:77
  245.2 183.2 %all-reduce.8.cloned.1.call-start = ((), (), s32[]{:S(2)}) async-start(), calls=%async_computation.7 | async-start | bytes 4194304 | tf_op jit(solution)/shard_map/psum | solution.py:63
  252.1 225.2 %all-reduce.4.cloned.1.call-start = ((), (), s32[]{:S(2)}) async-start(), calls=%async_computation.5 | async-start | bytes 524288 | tf_op jit(solution)/shard_map/psum | solution.py:85
  284.5 4.7 copy-start.4
  285.2 1.9 copy-start.1
  287.2 190.1 %collective-permute-start.1 = (f32[4,1,128]{2,0,1:T(4,128)S(1)}, f32[4,1,128]{2,0,1:T(4,128)S(1)}, u32[]{:S(2)}, u32[]{:S(2)}) collective-permute-start(f32[4,1,128]{2,0,1:T(4,128)S(1)} %bitcast.91), channel_id=1, source_target_pairs={{0,16},{16,32},{32,48},{1,17},{17,33},{33,49},{2,18},{18,34},{34,5... | collective-permute-start | bytes 6152 | tf_op jit(solution)/shard_map/ppermute | solution.py:13
  290.7 238.0 %all-reduce.6.cloned.1.call-start = ((), (), s32[]{:S(2)}) async-start(), calls=%async_computation.6 | async-start | bytes 524288 | tf_op jit(solution)/shard_map/psum | solution.py:85
  428.4 4.4 copy-start.2
Sparse Core Ops, SparseCore 0:
  29.1 38.0 reduce-scatter.4
  69.0 79.0 all-gather.2
  165.0 78.3 reduce-scatter.6
  245.8 31.0 all-gather.4
  280.2 148.2 all-reduce.7
  431.3 45.9 all-reduce.3
  479.9 48.7 all-reduce.5
